TPU v7x, 512 devices: a whole 4x4x16 slice. The times are simulated.
512 devices in a mesh: row: 64 (over z_lo, x, core), col: 8 (over y, z_hi).
Axes of the slice: x: 4, y: 4, z: 16 (z_hi: 2, z_lo: 8; z = z_hi * 8 + z_lo), core: 2. Of those that a mesh axis runs over, the one named last changes fastest.
Arguments:
- u3: bfloat16 [2048, 64, 512], P(('row', 'col')), may hold values from -6 to 6
- g3: bfloat16 [2048, 64, 512], P(('row', 'col')), may hold values from -6 to 6
- ln3_w: float32 [512], replicated, may hold values from 0.25 to 1.75
- ln3_b: float32 [512], replicated, may hold values from -3 to 3
- bias3: float32 [2048], replicated, may hold values from -3 to 3
- gamma3: float32 [512], replicated, may hold values from 0.3 to 1.5
- kernel3: float32 [7, 7, 512], replicated, may hold values from -0.875 to 0.875
- expand3: bfloat16 [512, 2048], P(None, 'row'), may hold values from -0.25 to 0.25
- project3: bfloat16 [512, 2048], P(None, 'row'), may hold values from -0.125 to 0.125
- down_w: bfloat16 [1024, 512], P(None, 'row'), may hold values from -0.1875 to 0.1875
- dln_w: float32 [256], replicated, may hold values from 0.25 to 1.75
- y2: bfloat16 [4096, 128, 256], P('row', 'col'), may hold values from -6 to 6
- u2: bfloat16 [4096, 128, 256], P('row', 'col'), may hold values from -6 to 6
- ln2_w: float32 [256], replicated, may hold values from 0.25 to 1.75
- ln2_b: float32 [256], replicated, may hold values from -3 to 3
- bias2: float32 [1024], replicated, may hold values from -3 to 3
- gamma2: float32 [256], replicated, may hold values from 0.3 to 1.5
- kernel2: float32 [7, 7, 256], replicated, may hold values from -0.875 to 0.875
- expand2: bfloat16 [256, 1024], P(None, 'row'), may hold values from -0.375 to 0.375
- project2: bfloat16 [256, 1024], P(None, 'row'), may hold values from -0.1875 to 0.1875
- tissue: int32 [256, 8], P('row', 'col'), may hold values 0 or 1
Outputs:
- gx2: bfloat16 [4096, 128, 256], P('row', 'col')
Inputs may be any that keep to these rules, and one draw needn't show every extreme that they name: tissue marks tiles holding tissue.
All inputs are finite; a program needn't handle non-finite values. No bound on the sum of `tissue` on one device may be relied on, other than what follows from the above.
Results may differ from a plain program's by a relative error of at most 0.014.
Values may be sent and summed in bfloat16 or wider, within the bound.
No kernel may reach another device: no remote copies, remote signals or barrier semaphores. Data moves between devices by JAX's collectives and lax.ppermute only.
A program may use at most 64 MiB of HBM per device.

v0:
```python
import jax
import jax.numpy as jnp
from jax import lax
from jax.sharding import PartitionSpec as P

TILE = 16
EPS = 1e-06
ROOT_HALF = 0.7071067811865476
DENS = 0.3989422804014327


def padded_2(block, sides, width):
    for axis, dim in sides:
        count = lax.axis_size(axis)
        forward = [(i, i + 1) for i in range(count - 1)]
        backward = [(target, source) for source, target in forward]
        low = lax.ppermute(
            lax.slice_in_dim(block, block.shape[dim] - width, None, axis=dim), axis, forward
        )
        high = lax.ppermute(lax.slice_in_dim(block, 0, width, axis=dim), axis, backward)
        block = jnp.concatenate([low, block, high], axis=dim)
    return block


def block_grad(u, g, layernorm_weight, layernorm_bias, bias, gamma, expand, project):
    count = u.shape[0]
    width = u.shape[1]
    blk = min(count, 512)

    def one(pair):
        ub, gb = pair
        uf = ub.astype(jnp.float32)
        centered_input = uf - jnp.mean(uf, axis=-1, keepdims=True)
        inverse_deviation = lax.rsqrt(
            jnp.mean(centered_input * centered_input, axis=-1, keepdims=True) + EPS
        )
        standardized_input = centered_input * inverse_deviation
        normalized_output = (standardized_input * layernorm_weight + layernorm_bias).astype(
            jnp.bfloat16
        )
        hidden = jnp.dot(normalized_output, expand, preferred_element_type=jnp.float32) + bias
        scaled = (gamma * gb.astype(jnp.float32)).astype(jnp.bfloat16)
        grad_act = jnp.dot(scaled, project, preferred_element_type=jnp.float32)
        slope = 0.5 * (1.0 + jax.scipy.special.erf(hidden * ROOT_HALF)) + hidden * DENS * jnp.exp(
            -0.5 * hidden * hidden
        )
        grad_hid = (grad_act * slope).astype(jnp.bfloat16)
        grad_norm = lax.dot_general(
            grad_hid, expand, (((1,), (1,)), ((), ())), preferred_element_type=jnp.float32
        )
        projection_term = grad_norm * layernorm_weight
        upstream_gradient = inverse_deviation * (
            projection_term
            - jnp.mean(projection_term, axis=-1, keepdims=True)
            - standardized_input
            * jnp.mean(projection_term * standardized_input, axis=-1, keepdims=True)
        )
        return upstream_gradient.astype(jnp.bfloat16)

    result = lax.map(
        one, (u.reshape(count // blk, blk, width), g.reshape(count // blk, blk, width))
    )
    return result.reshape(count, width)


def spread(padded, kernel, height, width):
    total = jnp.zeros((height, width, padded.shape[2]), jnp.float32)
    for dy in range(7):
        for dx in range(7):
            total = total + kernel[dy, dx] * padded[
                6 - dy : 6 - dy + height, 6 - dx : 6 - dx + width
            ].astype(jnp.float32)
    return total


def norm_back(value, grad, gain):
    vf = value.astype(jnp.float32)
    centered_input = vf - jnp.mean(vf, axis=-1, keepdims=True)
    inverse_deviation = lax.rsqrt(
        jnp.mean(centered_input * centered_input, axis=-1, keepdims=True) + EPS
    )
    yhat = centered_input * inverse_deviation
    projection_term = grad * gain
    return inverse_deviation * (
        projection_term
        - jnp.mean(projection_term, axis=-1, keepdims=True)
        - yhat * jnp.mean(projection_term * yhat, axis=-1, keepdims=True)
    )


def project_down(grads, down_whole):
    return lax.dot_general(
        grads, down_whole, (((1,), (1,)), ((), ())), preferred_element_type=jnp.float32
    )


def on_device(
    u3,
    g3,
    ln3_w,
    ln3_b,
    bias3,
    gamma3,
    kernel3,
    expand3,
    project3,
    down_w,
    dln_w,
    y2,
    u2,
    ln2_w,
    ln2_b,
    bias2,
    gamma2,
    kernel2,
    expand2,
    project2,
    tissue,
):
    expand3, project3, down_w, expand2, project2 = (
        lax.all_gather(expand3, "row", axis=1, tiled=True),
        lax.all_gather(project3, "row", axis=1, tiled=True),
        lax.all_gather(down_w, "row", axis=1, tiled=True),
        lax.all_gather(expand2, "row", axis=1, tiled=True),
        lax.all_gather(project2, "row", axis=1, tiled=True),
    )
    rows3, width3, chans3 = u3.shape
    rows2, cols2, chans2 = y2.shape
    grad_u3 = block_grad(
        u3.reshape(-1, chans3),
        g3.reshape(-1, chans3),
        ln3_w,
        ln3_b,
        bias3,
        gamma3,
        expand3,
        project3,
    ).reshape(u3.shape)
    rimmed3 = padded_2(grad_u3, ((("row", "col"), 0),), 3)
    padded3 = jnp.pad(rimmed3, ((0, 0), (3, 3), (0, 0)))
    gx3 = (g3.astype(jnp.float32) + spread(padded3, kernel3, rows3, width3)).astype(jnp.bfloat16)
    grad_m = project_down(gx3.reshape(-1, chans3), down_w).astype(jnp.bfloat16)
    grad_m = grad_m.reshape(rows3, width3, 4 * chans2)
    moved = lax.all_to_all(grad_m, "col", split_axis=1, concat_axis=0, tiled=True)
    grad_mf = moved.astype(jnp.float32)
    grad_mf = (
        grad_mf.reshape(rows2 // 2, cols2 // 2, 2, 2, chans2)
        .transpose(0, 2, 1, 3, 4)
        .reshape(rows2, cols2, chans2)
    )
    grad_y = norm_back(y2, grad_mf, dln_w)
    tile_rows, tile_cols = tissue.shape
    pixel_mask = jnp.broadcast_to(
        tissue.astype(jnp.float32)[:, None, :, None], (tile_rows, TILE, tile_cols, TILE)
    ).reshape(rows2, cols2)
    g2 = (grad_y * pixel_mask[:, :, None]).astype(jnp.bfloat16)
    grad_u2 = block_grad(
        u2.reshape(-1, chans2),
        g2.reshape(-1, chans2),
        ln2_w,
        ln2_b,
        bias2,
        gamma2,
        expand2,
        project2,
    ).reshape(u2.shape)
    padded2 = padded_2(grad_u2, (("row", 0), ("col", 1)), 3)
    return (g2.astype(jnp.float32) + spread(padded2, kernel2, rows2, cols2)).astype(jnp.bfloat16)


def solution(mesh):
    placed = (
        P(("row", "col"), None, None),
        P(("row", "col"), None, None),
        P(),
        P(),
        P(),
        P(),
        P(),
        P(None, "row"),
        P(None, "row"),
        P(None, "row"),
        P(),
        P("row", "col", None),
        P("row", "col", None),
        P(),
        P(),
        P(),
        P(),
        P(),
        P(None, "row"),
        P(None, "row"),
        P("row", "col"),
    )
    return jax.shard_map(
        on_device, mesh=mesh, in_specs=placed, out_specs=P("row", "col", None), check_vma=False
    )
```

profile of v0, /device:TPU:10, one launch (start us, length us, event | category | flops | bytes accessed | tf_op | source)
XLA Modules:
  0.0 729.9 jit_solution(1171352033100653243)
XLA Ops:
  15.6 118.1 %all-gather.6.cloned.1.call-done = bf16[512,2048]{0,1:T(8,128)(2,1)} async-done(((bf16[512,32]{0,1:T(8,128)(2,1)}), bf16[512,2048]{0,1:T(8,128)(2,1)}) %all-gather.6.cloned.1.call-update) | async-done | bytes 2097168 | tf_op jit(solution)/shard_map/all_gather | solution.py:121
  133.7 3.8 convolution_add_fusion
  137.6 114.7 %all-gather.4.cloned.1.call-done = bf16[512,2048]{0,1:T(8,128)(2,1)} async-done(((bf16[512,32]{0,1:T(8,128)(2,1)}), bf16[512,2048]{0,1:T(8,128)(2,1)}) %all-gather.4.cloned.1.call-update) | async-done | bytes 2097168 | tf_op jit(solution)/shard_map/all_gather | solution.py:122
  252.3 4.1 fusion.90
  256.7 8.3 %collective-permute-start = (bf16[3,64,512]{2,1,0:T(8,128)(2,1)S(1)}, bf16[3,64,512]{2,1,0:T(8,128)(2,1)S(1)}, u32[]{:S(2)}, u32[]{:S(2)}) collective-permute-start(bf16[3,64,512]{2,1,0:T(8,128)(2,1)S(1)} %bitcast.212), channel_id=1, source_target_pairs={{0,1},{1,2},{2,3},{3,4},{4,5},{5,6},{6,7},{7,8},{8,9},{9,10},{10,1... | collective-permute-start | bytes 589832 | tf_op jit(solution)/shard_map/ppermute | solution.py:17
  265.0 7.2 collective-permute-start.1
  273.1 14.7 %collective-permute-done = bf16[3,64,512]{2,1,0:T(8,128)(2,1)S(1)} collective-permute-done((bf16[3,64,512]{2,1,0:T(8,128)(2,1)S(1)}, bf16[3,64,512]{2,1,0:T(8,128)(2,1)S(1)}, u32[]{:S(2)}, u32[]{:S(2)}) %collective-permute-start) | collective-permute-done | bytes 196640 | tf_op jit(solution)/shard_map/ppermute | solution.py:17
  287.8 10.1 %collective-permute-done.1 = bf16[3,64,512]{2,1,0:T(8,128)(2,1)S(1)} collective-permute-done((bf16[3,64,512]{2,1,0:T(8,128)(2,1)S(1)}, bf16[3,64,512]{2,1,0:T(8,128)(2,1)S(1)}, u32[]{:S(2)}, u32[]{:S(2)}) %collective-permute-start.1) | collective-permute-done | bytes 196640 | tf_op jit(solution)/shard_map/ppermute | solution.py:20
  298.1 4.0 add_convert_fusion.1
  302.1 90.6 %all-gather.8.cloned.1.call-done = bf16[1024,512]{0,1:T(8,128)(2,1)} async-done(((bf16[1024,8]{0,1:T(8,128)(2,1)}), bf16[1024,512]{0,1:T(8,128)(2,1)}) %all-gather.8.cloned.1.call-update) | async-done | bytes 1048592 | tf_op jit(solution)/shard_map/all_gather | solution.py:123
  395.6 12.2 %all-to-all-start = ((bf16[4,64,1024]{2,0,1:T(4,128)(2,1)}), bf16[4,64,1024]{2,0,1:T(4,128)(2,1)S(1)}, u32[]{:S(2)}, u32[]{:S(2)}) async-start(bf16[4,64,1024]{2,0,1:T(4,128)(2,1)} %copy.47), calls=%async_computation | async-start | bytes 1048576 | tf_op jit(solution)/shard_map/all_to_all | solution.py:144
  408.5 119.2 %all_gather.18 = bf16[256,1024]{0,1:T(8,128)(2,1)S(1)} all-gather(bf16[256,16]{0,1:T(8,128)(2,1)S(1)} %copy-done.8), channel_id=1, replica_groups=mesh['row'=64,'col'=8] {'row'}, dimensions={1}, use_global_device_ids=true | all-gather | bytes 532480 | tf_op jit(solution)/shard_map/all_gather | solution.py:125
  527.9 118.3 %all_gather.19 = bf16[256,1024]{0,1:T(8,128)(2,1)S(1)} all-gather(bf16[256,16]{0,1:T(8,128)(2,1)S(1)} %copy-done.9), channel_id=1, replica_groups=mesh['row'=64,'col'=8] {'row'}, dimensions={1}, use_global_device_ids=true | all-gather | bytes 532480 | tf_op jit(solution)/shard_map/all_gather | solution.py:124
  651.2 1.9 reshape.128
  656.6 13.0 %while.2 = (s32[]{:T(128)}, bf16[2,512,256]{2,1,0:T(8,128)(2,1)}, bf16[2,512,256]{2,1,0:T(8,128)(2,1)}, f32[256]{0:T(256)S(1)}, bf16[2,512,256]{2,1,0:T(8,128)(2...) while((s32[]{:T(128)}, bf16[2,512,256]{2,1,0:T(8,128)(2,1)}, ...), condition=%wide.region_13.14_spmd, body=%wide.region_8.13_spmd.sunk | while | flops 815006208 | bytes 10033349 | solution.py:60
  659.4 2.7 fusion.127
  665.9 2.7 fusion.127
  670.6 2.2 collective-permute-start.2
  672.8 3.3 collective-permute-start.3
  678.8 14.1 %collective-permute-start.4 = (bf16[70,3,256]{2,1,0:T(4,128)(2,1)S(1)}, bf16[70,3,256]{2,1,0:T(4,128)(2,1)S(1)}, u32[]{:S(2)}, u32[]{:S(2)}) collective-permute-start(bf16[70,3,256]{2,1,0:T(4,128)(2,1)S(1)} %get-tuple-element.157), channel_id=1, source_target_pairs={{1,0},{2,1},{3,2},{4,3},{5,4},{6,5},{7,6},{9,8},{10,9},{11,10},{12... | collective-permute-start | bytes 322568 | tf_op jit(solution)/shard_map/ppermute | solution.py:20
  692.9 1.9 collective-permute-start.5
  694.9 2.2 collective-permute-done.4
  697.0 13.1 %collective-permute-done.5 = bf16[70,3,256]{2,1,0:T(4,128)(2,1)S(1)} collective-permute-done((bf16[70,3,256]{2,1,0:T(4,128)(2,1)S(1)}, bf16[70,3,256]{2,1,0:T(4,128)(2,1)S(1)}, u32[]{:S(2)}, u32[]{:S(2)}) %collective-permute-start.5) | collective-permute-done | bytes 107552 | tf_op jit(solution)/shard_map/ppermute | solution.py:17
  712.0 11.3 %add_convert_fusion = bf16[64,16,256]{2,1,0:T(8,128)(2,1)} fusion(bf16[64,16,256]{2,1,0:T(8,128)(2,1)S(1)} %bitcast.207, bf16[64,16,256]{2,1,0:T(8,128)(2,1)} %fusion.62, bf16[3,16,256]{2,1,0:T(8,128)(2,1)S(1)} %collective-permute-done.2, bf16[3,16,256]{2,1,0:T(8,128)(2,1)S(1)} %collective-permute-done.3, bf16[70,19,256]{2,1,0:T(8,128)(2,1)S(1)} %get-tuple-element.156, ...), kind=kLoop, calls=%fused_computation.77 | loop fusion | flops 40632320 | bytes 23692288 | tf_op jit(solution)/shard_map/convert_element_type | solution.py:168
  (144 shorter events, 35.1 us)
Async XLA Ops:
  6.5 127.2 %all-gather.6.cloned.1.call-start = ((), (), s32[]{:S(2)}) async-start(), calls=%async_computation.2 | async-start | bytes 2129920 | tf_op jit(solution)/shard_map/all_gather | solution.py:121
  7.3 245.1 %all-gather.4.cloned.1.call-start = ((), (), s32[]{:S(2)}) async-start(), calls=%async_computation.1 | async-start | bytes 2129920 | tf_op jit(solution)/shard_map/all_gather | solution.py:122
  8.0 384.6 %all-gather.8.cloned.1.call-start = ((), (), s32[]{:S(2)}) async-start(), calls=%async_computation.3 | async-start | bytes 1064960 | tf_op jit(solution)/shard_map/all_gather | solution.py:123
  15.6 236.8 %copy-start.2 = (bf16[4,64,512]{2,1,0:T(8,128)(2,1)S(1)}, bf16[4,64,512]{2,1,0:T(8,128)(2,1)}, u32[]{:S(2)}) copy-start(bf16[4,64,512]{2,1,0:T(8,128)(2,1)} %param.23) | copy-start | bytes 786436
  15.6 236.8 %copy-start.25 = (f32[512]{0:T(512)S(1)}, f32[512]{0:T(512)}, u32[]{:S(2)}) copy-start(f32[512]{0:T(512)} %param.25) | copy-start | bytes 6148
  133.7 118.6 %copy-start.3 = (bf16[512,2048]{0,1:T(8,128)(2,1)S(1)}, bf16[512,2048]{0,1:T(8,128)(2,1)}, u32[]{:S(2)}) copy-start(bf16[512,2048]{0,1:T(8,128)(2,1)} %all-gather.6.cloned.1.call-done) | copy-start | bytes 6291460
  256.7 31.1 %collective-permute-start = (bf16[3,64,512]{2,1,0:T(8,128)(2,1)S(1)}, bf16[3,64,512]{2,1,0:T(8,128)(2,1)S(1)}, u32[]{:S(2)}, u32[]{:S(2)}) collective-permute-start(bf16[3,64,512]{2,1,0:T(8,128)(2,1)S(1)} %bitcast.212), channel_id=1, source_target_pairs={{0,1},{1,2},{2,3},{3,4},{4,5},{5,6},{6,7},{7,8},{8,9},{9,10},{10,1... | collective-permute-start | bytes 589832 | tf_op jit(solution)/shard_map/ppermute | solution.py:17
  265.0 32.9 %collective-permute-start.1 = (bf16[3,64,512]{2,1,0:T(8,128)(2,1)S(1)}, bf16[3,64,512]{2,1,0:T(8,128)(2,1)S(1)}, u32[]{:S(2)}, u32[]{:S(2)}) collective-permute-start(bf16[3,64,512]{2,1,0:T(8,128)(2,1)S(1)} %bitcast.211), channel_id=1, source_target_pairs={{1,0},{2,1},{3,2},{4,3},{5,4},{6,5},{7,6},{8,7},{9,8},{10,9},{11,1... | collective-permute-start | bytes 589832 | tf_op jit(solution)/shard_map/ppermute | solution.py:20
  302.1 105.7 %copy-start.30 = (s32[4,1]{0,1:T(1,128)S(1)}, s32[4,1]{0,1:T(1,128)}, u32[]{:S(2)}) copy-start(s32[4,1]{0,1:T(1,128)} %param.43) | copy-start | bytes 52
  302.1 106.4 %copy-start.8 = (bf16[256,16]{0,1:T(8,128)(2,1)S(1)}, bf16[256,16]{0,1:T(8,128)(2,1)}, u32[]{:S(2)}) copy-start(bf16[256,16]{0,1:T(8,128)(2,1)} %param.42) | copy-start | bytes 24580
  394.3 133.6 %copy-start.9 = (bf16[256,16]{0,1:T(8,128)(2,1)S(1)}, bf16[256,16]{0,1:T(8,128)(2,1)}, u32[]{:S(2)}) copy-start(bf16[256,16]{0,1:T(8,128)(2,1)} %param.41) | copy-start | bytes 24580
  395.5 251.7 %copy-start = (bf16[64,16,256]{2,1,0:T(8,128)(2,1)S(1)}, bf16[64,16,256]{2,1,0:T(8,128)(2,1)}, u32[]{:S(2)}) copy-start(bf16[64,16,256]{2,1,0:T(8,128)(2,1)} %param.34) | copy-start | bytes 1572868
  395.6 253.0 %all-to-all-start = ((bf16[4,64,1024]{2,0,1:T(4,128)(2,1)}), bf16[4,64,1024]{2,0,1:T(4,128)(2,1)S(1)}, u32[]{:S(2)}, u32[]{:S(2)}) async-start(bf16[4,64,1024]{2,0,1:T(4,128)(2,1)} %copy.47), calls=%async_computation | async-start | bytes 1048576 | tf_op jit(solution)/shard_map/all_to_all | solution.py:144
  408.5 239.4 %copy-start.5 = (f32[7,7,256]{2,1,0:T(8,128)S(1)}, f32[7,7,256]{2,1,0:T(8,128)}, u32[]{:S(2)}) copy-start(f32[7,7,256]{2,1,0:T(8,128)} %param.40) | copy-start | bytes 150532
  669.6 42.3 %copy-start.13 = (f32[1,1,256]{2,1,0:T(1,128)S(1)}, f32[1,1,256]{2,1,0:T(1,128)}, u32[]{:S(2)}) copy-start(f32[1,1,256]{2,1,0:T(1,128)} %get-tuple-element.219) | copy-start | bytes 3076
  669.6 42.3 %copy-start.14 = (f32[1,1,256]{2,1,0:T(1,128)S(1)}, f32[1,1,256]{2,1,0:T(1,128)}, u32[]{:S(2)}) copy-start(f32[1,1,256]{2,1,0:T(1,128)} %get-tuple-element.220) | copy-start | bytes 3076
  669.6 42.3 %copy-start.15 = (f32[1,1,256]{2,1,0:T(1,128)S(1)}, f32[1,1,256]{2,1,0:T(1,128)}, u32[]{:S(2)}) copy-start(f32[1,1,256]{2,1,0:T(1,128)} %get-tuple-element.221) | copy-start | bytes 3076
  669.7 42.3 %copy-start.16 = (f32[1,1,256]{2,1,0:T(1,128)S(1)}, f32[1,1,256]{2,1,0:T(1,128)}, u32[]{:S(2)}) copy-start(f32[1,1,256]{2,1,0:T(1,128)} %get-tuple-element.222) | copy-start | bytes 3076
  669.7 42.3 %copy-start.17 = (f32[1,1,256]{2,1,0:T(1,128)S(1)}, f32[1,1,256]{2,1,0:T(1,128)}, u32[]{:S(2)}) copy-start(f32[1,1,256]{2,1,0:T(1,128)} %get-tuple-element.223) | copy-start | bytes 3076
  669.7 42.3 %copy-start.18 = (f32[1,1,256]{2,1,0:T(1,128)S(1)}, f32[1,1,256]{2,1,0:T(1,128)}, u32[]{:S(2)}) copy-start(f32[1,1,256]{2,1,0:T(1,128)} %get-tuple-element.224) | copy-start | bytes 3076
  670.6 5.6 collective-permute-start.2
  672.8 4.8 collective-permute-start.3
  678.8 18.2 %collective-permute-start.4 = (bf16[70,3,256]{2,1,0:T(4,128)(2,1)S(1)}, bf16[70,3,256]{2,1,0:T(4,128)(2,1)S(1)}, u32[]{:S(2)}, u32[]{:S(2)}) collective-permute-start(bf16[70,3,256]{2,1,0:T(4,128)(2,1)S(1)} %get-tuple-element.157), channel_id=1, source_target_pairs={{1,0},{2,1},{3,2},{4,3},{5,4},{6,5},{7,6},{9,8},{10,9},{11,10},{12... | collective-permute-start | bytes 322568 | tf_op jit(solution)/shard_map/ppermute | solution.py:20
  692.9 17.2 %collective-permute-start.5 = (bf16[70,3,256]{2,1,0:T(4,128)(2,1)S(1)}, bf16[70,3,256]{2,1,0:T(4,128)(2,1)S(1)}, u32[]{:S(2)}, u32[]{:S(2)}) collective-permute-start(bf16[70,3,256]{2,1,0:T(4,128)(2,1)S(1)} %get-tuple-element.158), channel_id=1, source_target_pairs={{0,1},{1,2},{2,3},{3,4},{4,5},{5,6},{6,7},{8,9},{9,10},{10,11},{11... | collective-permute-start | bytes 322568 | tf_op jit(solution)/shard_map/ppermute | solution.py:17
  (20 other events, 481.8 us)
Sparse Core Ops, SparseCore 0:
  9.5 124.2 all-gather.5
  135.9 116.3 all-gather.3
  254.5 138.1 all-gather.7
where the time goes:
time: 731 us; the launch traced here: 730 us
  waiting for transfers between devices  367 us (50%)
  blocking collectives  238 us (33%)
  starting transfers between devices  49.3 us (7%)
  other arithmetic  27.2 us (4%)
  matrix products  17.8 us (2%)
  local copies, waits for them, and re-layouts  17.1 us (2%)
  between operations  13.7 us (2%)
    all_gather x1, blocking collectives, on_device(): lax.all_gather(project2, 'row', axis=1, tiled=True)  119 us
    all_gather x1, blocking collectives, on_device(): lax.all_gather(expand2, 'row', axis=1, tiled=True)  118 us
    all_gather x1, waiting for transfers between devices, on_device(): lax.all_gather(expand3, 'row', axis=1, tiled=True)  118 us
    all_gather x1, waiting for transfers between devices, on_device(): lax.all_gather(project3, 'row', axis=1, tiled=True)  115 us
    all_gather x1, waiting for transfers between devices, on_device(): lax.all_gather(down_w, 'row', axis=1, tiled=True)  90.6 us
    ppermute x3, waiting for transfers between devices, padded_2(): lax.ppermute(lax.slice_in_dim(block, block.shape[dim] - width, None, axis...  27.8 us
    ppermute x3, starting transfers between devices, padded_2(): lax.ppermute(lax.slice_in_dim(block, 0, width, axis=dim), axis, backward)  24.6 us
  transfers between devices with their start and end apart: 10, of which 8 were waited for; matrix products, arithmetic and copies ran while one was open for 3% of the time, Pallas kernels for 0%

commit v1 on v0

--- a/solution.py
+++ b/solution.py
@@ -121,7 +121,9 @@
         lax.all_gather(expand3, "row", axis=1, tiled=True),
         lax.all_gather(project3, "row", axis=1, tiled=True),
         lax.all_gather(down_w, "row", axis=1, tiled=True),
-        lax.all_gather(expand2, "row", axis=1, tiled=True),
+        jnp.concatenate(
+            lax.all_to_all(jnp.stack([expand2] * lax.axis_size("row")), "row", 0, 0), axis=1
+        ),
         lax.all_gather(project2, "row", axis=1, tiled=True),
     )
     rows3, width3, chans3 = u3.shape

time: 731 us -> 623 us (0.85)
  blocking collectives: 238 us -> 122 us
  starting transfers between devices: 49.3 us -> 66.9 us
  waiting for transfers between devices: 367 us -> 357 us
    all_gather x1 -> x0, blocking collectives: 118 us -> none  [on_device(): lax.all_gather(expand2, 'row', axis=1, tiled=True)]
    all_to_all x0 -> x1, starting transfers between devices: none -> 16.1 us  [on_device(): lax.all_to_all(jnp.stack([expand2] * lax.axis_size('row')), 'row', 0, 0)]
    all_gather x1, waiting for transfers between devices: 118 us -> 107 us  [on_device(): lax.all_gather(expand3, 'row', axis=1, tiled=True)]
  transfers between devices with their start and end apart: 10 -> 11, of which waited for: 8 -> 8; matrix products, arithmetic and copies ran while one was open for 3% -> 4% of each run, Pallas kernels for 0% -> 0%
where the time goes in v1:
time: 623 us; the launch traced here: 622 us
  waiting for transfers between devices  357 us (57%)
  blocking collectives  122 us (20%)
  starting transfers between devices  66.9 us (11%)
  other arithmetic  26.1 us (4%)
  matrix products  18.6 us (3%)
  local copies, waits for them, and re-layouts  16.9 us (3%)
  between operations  14.2 us (2%)
    all_gather x1, blocking collectives, on_device(): lax.all_gather(project2, 'row', axis=1, tiled=True)  122 us
    all_gather x1, waiting for transfers between devices, on_device(): lax.all_gather(project3, 'row', axis=1, tiled=True)  117 us
    all_gather x1, waiting for transfers between devices, on_device(): lax.all_gather(expand3, 'row', axis=1, tiled=True)  107 us
    all_gather x1, waiting for transfers between devices, on_device(): lax.all_gather(down_w, 'row', axis=1, tiled=True)  89.9 us
    ppermute x3, waiting for transfers between devices, padded_2(): lax.ppermute(lax.slice_in_dim(block, block.shape[dim] - width, None, axis...  28.4 us
    ppermute x3, starting transfers between devices, padded_2(): lax.ppermute(lax.slice_in_dim(block, 0, width, axis=dim), axis, backward)  24.4 us
    all_to_all x1, starting transfers between devices, on_device(): lax.all_to_all(jnp.stack([expand2] * lax.axis_size('row')), 'row', 0, 0)  16.1 us
    ppermute x3, starting transfers between devices, padded_2(): lax.ppermute(lax.slice_in_dim(block, block.shape[dim] - width, None, axis...  14.2 us
  transfers between devices with their start and end apart: 11, of which 8 were waited for; matrix products, arithmetic and copies ran while one was open for 4% of the time, Pallas kernels for 0%

profile of v1, /device:TPU:10, one launch (start us, length us, event | category | flops | bytes accessed | tf_op | source)
XLA Modules:
  0.0 622.1 jit_solution(12136753431146917190)
XLA Ops:
  9.6 16.1 %all-to-all-start.1 = ((bf16[64,256,16]{1,2,0:T(8,128)(2,1)}), bf16[64,256,16]{1,2,0:T(8,128)(2,1)S(1)}, u32[]{:S(2)}, u32[]{:S(2)}) async-start(bf16[64,256,16]{1,2,0:T(8,128)(2,1)} %stack.2), calls=%async_computation.1 | async-start | bytes 1048576 | tf_op jit(solution)/shard_map/all_to_all | solution.py:125
  30.2 107.1 %all-gather.6.cloned.1.call-done = bf16[512,2048]{0,1:T(8,128)(2,1)} async-done(((bf16[512,32]{0,1:T(8,128)(2,1)}), bf16[512,2048]{0,1:T(8,128)(2,1)}) %all-gather.6.cloned.1.call-update) | async-done | bytes 2097168 | tf_op jit(solution)/shard_map/all_gather | solution.py:121
  137.3 3.8 convolution_add_fusion
  141.2 117.0 %all-gather.4.cloned.1.call-done = bf16[512,2048]{0,1:T(8,128)(2,1)} async-done(((bf16[512,32]{0,1:T(8,128)(2,1)}), bf16[512,2048]{0,1:T(8,128)(2,1)}) %all-gather.4.cloned.1.call-update) | async-done | bytes 2097168 | tf_op jit(solution)/shard_map/all_gather | solution.py:122
  258.2 4.9 fusion.90
  264.7 8.2 %collective-permute-start = (bf16[3,64,512]{2,1,0:T(8,128)(2,1)S(1)}, bf16[3,64,512]{2,1,0:T(8,128)(2,1)S(1)}, u32[]{:S(2)}, u32[]{:S(2)}) collective-permute-start(bf16[3,64,512]{2,1,0:T(8,128)(2,1)S(1)} %bitcast.216), channel_id=1, source_target_pairs={{0,1},{1,2},{2,3},{3,4},{4,5},{5,6},{6,7},{7,8},{8,9},{9,10},{10,1... | collective-permute-start | bytes 589832 | tf_op jit(solution)/shard_map/ppermute | solution.py:17
  273.0 7.2 %collective-permute-start.1 = (bf16[3,64,512]{2,1,0:T(8,128)(2,1)S(1)}, bf16[3,64,512]{2,1,0:T(8,128)(2,1)S(1)}, u32[]{:S(2)}, u32[]{:S(2)}) collective-permute-start(bf16[3,64,512]{2,1,0:T(8,128)(2,1)S(1)} %bitcast.215), channel_id=1, source_target_pairs={{1,0},{2,1},{3,2},{4,3},{5,4},{6,5},{7,6},{8,7},{9,8},{10,9},{11,1... | collective-permute-start | bytes 589832 | tf_op jit(solution)/shard_map/ppermute | solution.py:20
  280.2 15.8 %collective-permute-done = bf16[3,64,512]{2,1,0:T(8,128)(2,1)S(1)} collective-permute-done((bf16[3,64,512]{2,1,0:T(8,128)(2,1)S(1)}, bf16[3,64,512]{2,1,0:T(8,128)(2,1)S(1)}, u32[]{:S(2)}, u32[]{:S(2)}) %collective-permute-start) | collective-permute-done | bytes 196640 | tf_op jit(solution)/shard_map/ppermute | solution.py:17
  296.0 10.4 %collective-permute-done.1 = bf16[3,64,512]{2,1,0:T(8,128)(2,1)S(1)} collective-permute-done((bf16[3,64,512]{2,1,0:T(8,128)(2,1)S(1)}, bf16[3,64,512]{2,1,0:T(8,128)(2,1)S(1)}, u32[]{:S(2)}, u32[]{:S(2)}) %collective-permute-start.1) | collective-permute-done | bytes 196640 | tf_op jit(solution)/shard_map/ppermute | solution.py:20
  307.0 4.0 add_convert_fusion.1
  311.0 89.9 %all-gather.8.cloned.1.call-done = bf16[1024,512]{0,1:T(8,128)(2,1)} async-done(((bf16[1024,8]{0,1:T(8,128)(2,1)}), bf16[1024,512]{0,1:T(8,128)(2,1)}) %all-gather.8.cloned.1.call-update) | async-done | bytes 1048592 | tf_op jit(solution)/shard_map/all_gather | solution.py:123
  403.7 12.2 %all-to-all-start = ((bf16[4,64,1024]{2,0,1:T(4,128)(2,1)}), bf16[4,64,1024]{2,0,1:T(4,128)(2,1)S(1)}, u32[]{:S(2)}, u32[]{:S(2)}) async-start(bf16[4,64,1024]{2,0,1:T(4,128)(2,1)} %copy.47), calls=%async_computation | async-start | bytes 1048576 | tf_op jit(solution)/shard_map/all_to_all | solution.py:146
  416.7 121.9 %all_gather.15 = bf16[256,1024]{0,1:T(8,128)(2,1)S(1)} all-gather(bf16[256,16]{0,1:T(8,128)(2,1)S(1)} %copy-done.10), channel_id=1, replica_groups=mesh['row'=64,'col'=8] {'row'}, dimensions={1}, use_global_device_ids=true | all-gather | bytes 532480 | tf_op jit(solution)/shard_map/all_gather | solution.py:127
  543.8 1.9 reshape.136
  549.2 13.0 %while.2 = (s32[]{:T(128)}, bf16[2,512,256]{2,1,0:T(8,128)(2,1)}, bf16[2,512,256]{2,1,0:T(8,128)(2,1)}, f32[256]{0:T(256)S(1)}, bf16[2,512,256]{2,1,0:T(8,128)(2...) while((s32[]{:T(128)}, bf16[2,512,256]{2,1,0:T(8,128)(2,1)}, ...), condition=%wide.region_13.14_spmd, body=%wide.region_8.13_spmd.sunk | while | flops 815006208 | bytes 10033349 | solution.py:60
  551.9 2.7 fusion.127
  558.4 2.7 fusion.127
  563.1 2.2 collective-permute-start.2
  565.4 6.0 collective-permute-start.3
  574.1 11.1 %collective-permute-start.4 = (bf16[70,3,256]{2,1,0:T(4,128)(2,1)S(1)}, bf16[70,3,256]{2,1,0:T(4,128)(2,1)S(1)}, u32[]{:S(2)}, u32[]{:S(2)}) collective-permute-start(bf16[70,3,256]{2,1,0:T(4,128)(2,1)S(1)} %get-tuple-element.157), channel_id=1, source_target_pairs={{1,0},{2,1},{3,2},{4,3},{5,4},{6,5},{7,6},{9,8},{10,9},{11,10},{12... | collective-permute-start | bytes 322568 | tf_op jit(solution)/shard_map/ppermute | solution.py:20
  585.2 3.7 collective-permute-start.5
  589.8 12.6 %collective-permute-done.5 = bf16[70,3,256]{2,1,0:T(4,128)(2,1)S(1)} collective-permute-done((bf16[70,3,256]{2,1,0:T(4,128)(2,1)S(1)}, bf16[70,3,256]{2,1,0:T(4,128)(2,1)S(1)}, u32[]{:S(2)}, u32[]{:S(2)}) %collective-permute-start.5) | collective-permute-done | bytes 107552 | tf_op jit(solution)/shard_map/ppermute | solution.py:17
  602.4 1.7 pad_maximum_fusion
  604.3 11.3 %add_convert_fusion = bf16[64,16,256]{2,1,0:T(8,128)(2,1)} fusion(bf16[64,16,256]{2,1,0:T(8,128)(2,1)S(1)} %bitcast.210, bf16[64,16,256]{2,1,0:T(8,128)(2,1)} %fusion.62, bf16[3,16,256]{2,1,0:T(8,128)(2,1)S(1)} %collective-permute-done.2, bf16[3,16,256]{2,1,0:T(8,128)(2,1)S(1)} %collective-permute-done.3, bf16[70,19,256]{2,1,0:T(8,128)(2,1)S(1)} %get-tuple-element.156, ...), kind=kLoop, calls=%fused_computation.77 | loop fusion | flops 40632320 | bytes 23692288 | tf_op jit(solution)/shard_map/convert_element_type | solution.py:170
  (220 shorter events, 33.0 us)
Async XLA Ops:
  6.6 130.8 %copy-start.9 = (f32[2048]{0:T(1024)S(1)}, f32[2048]{0:T(1024)}, u32[]{:S(2)}) copy-start(f32[2048]{0:T(1024)} %param.27) | copy-start | bytes 24580
  6.6 130.8 %all-gather.6.cloned.1.call-start = ((), (), s32[]{:S(2)}) async-start(), calls=%async_computation.3 | async-start | bytes 2129920 | tf_op jit(solution)/shard_map/all_gather | solution.py:121
  7.3 250.9 %all-gather.4.cloned.1.call-start = ((), (), s32[]{:S(2)}) async-start(), calls=%async_computation.2 | async-start | bytes 2129920 | tf_op jit(solution)/shard_map/all_gather | solution.py:122
  9.6 394.1 %all-to-all-start.1 = ((bf16[64,256,16]{1,2,0:T(8,128)(2,1)}), bf16[64,256,16]{1,2,0:T(8,128)(2,1)S(1)}, u32[]{:S(2)}, u32[]{:S(2)}) async-start(bf16[64,256,16]{1,2,0:T(8,128)(2,1)} %stack.2), calls=%async_computation.1 | async-start | bytes 1048576 | tf_op jit(solution)/shard_map/all_to_all | solution.py:125
  25.7 375.1 %all-gather.8.cloned.1.call-start = ((), (), s32[]{:S(2)}) async-start(), calls=%async_computation.4 | async-start | bytes 1064960 | tf_op jit(solution)/shard_map/all_gather | solution.py:123
  137.3 120.9 %copy-start.3 = (bf16[512,2048]{0,1:T(8,128)(2,1)S(1)}, bf16[512,2048]{0,1:T(8,128)(2,1)}, u32[]{:S(2)}) copy-start(bf16[512,2048]{0,1:T(8,128)(2,1)} %all-gather.6.cloned.1.call-done) | copy-start | bytes 6291460
  263.1 43.6 %copy-start.14 = (f32[1,1,512]{2,1,0:T(1,128)S(1)}, f32[1,1,512]{2,1,0:T(1,128)}, u32[]{:S(2)}) copy-start(f32[1,1,512]{2,1,0:T(1,128)} %get-tuple-element.189) | copy-start | bytes 6148
  263.1 43.6 %copy-start.15 = (f32[1,1,512]{2,1,0:T(1,128)S(1)}, f32[1,1,512]{2,1,0:T(1,128)}, u32[]{:S(2)}) copy-start(f32[1,1,512]{2,1,0:T(1,128)} %get-tuple-element.190) | copy-start | bytes 6148
  263.1 43.6 %copy-start.16 = (f32[1,1,512]{2,1,0:T(1,128)S(1)}, f32[1,1,512]{2,1,0:T(1,128)}, u32[]{:S(2)}) copy-start(f32[1,1,512]{2,1,0:T(1,128)} %get-tuple-element.191) | copy-start | bytes 6148
  263.1 43.6 %copy-start.17 = (f32[1,1,512]{2,1,0:T(1,128)S(1)}, f32[1,1,512]{2,1,0:T(1,128)}, u32[]{:S(2)}) copy-start(f32[1,1,512]{2,1,0:T(1,128)} %get-tuple-element.192) | copy-start | bytes 6148
  263.2 43.6 %copy-start.18 = (f32[1,1,512]{2,1,0:T(1,128)S(1)}, f32[1,1,512]{2,1,0:T(1,128)}, u32[]{:S(2)}) copy-start(f32[1,1,512]{2,1,0:T(1,128)} %get-tuple-element.193) | copy-start | bytes 6148
  263.2 43.6 %copy-start.19 = (f32[1,1,512]{2,1,0:T(1,128)S(1)}, f32[1,1,512]{2,1,0:T(1,128)}, u32[]{:S(2)}) copy-start(f32[1,1,512]{2,1,0:T(1,128)} %get-tuple-element.194) | copy-start | bytes 6148
  263.2 43.6 %copy-start.20 = (f32[1,1,512]{2,1,0:T(1,128)S(1)}, f32[1,1,512]{2,1,0:T(1,128)}, u32[]{:S(2)}) copy-start(f32[1,1,512]{2,1,0:T(1,128)} %get-tuple-element.195) | copy-start | bytes 6148
  264.7 31.3 %collective-permute-start = (bf16[3,64,512]{2,1,0:T(8,128)(2,1)S(1)}, bf16[3,64,512]{2,1,0:T(8,128)(2,1)S(1)}, u32[]{:S(2)}, u32[]{:S(2)}) collective-permute-start(bf16[3,64,512]{2,1,0:T(8,128)(2,1)S(1)} %bitcast.216), channel_id=1, source_target_pairs={{0,1},{1,2},{2,3},{3,4},{4,5},{5,6},{6,7},{7,8},{8,9},{9,10},{10,1... | collective-permute-start | bytes 589832 | tf_op jit(solution)/shard_map/ppermute | solution.py:17
  273.0 33.4 %collective-permute-start.1 = (bf16[3,64,512]{2,1,0:T(8,128)(2,1)S(1)}, bf16[3,64,512]{2,1,0:T(8,128)(2,1)S(1)}, u32[]{:S(2)}, u32[]{:S(2)}) collective-permute-start(bf16[3,64,512]{2,1,0:T(8,128)(2,1)S(1)} %bitcast.215), channel_id=1, source_target_pairs={{1,0},{2,1},{3,2},{4,3},{5,4},{6,5},{7,6},{8,7},{9,8},{10,9},{11,1... | collective-permute-start | bytes 589832 | tf_op jit(solution)/shard_map/ppermute | solution.py:20
  310.9 105.0 %copy-start.67 = (s32[4,1]{0,1:T(1,128)S(1)}, s32[4,1]{0,1:T(1,128)}, u32[]{:S(2)}) copy-start(s32[4,1]{0,1:T(1,128)} %param.43) | copy-start | bytes 52
  311.0 105.7 %copy-start.10 = (bf16[256,16]{0,1:T(8,128)(2,1)S(1)}, bf16[256,16]{0,1:T(8,128)(2,1)}, u32[]{:S(2)}) copy-start(bf16[256,16]{0,1:T(8,128)(2,1)} %param.42) | copy-start | bytes 24580
  402.5 136.3 %copy-start = (bf16[64,16,256]{2,1,0:T(8,128)(2,1)S(1)}, bf16[64,16,256]{2,1,0:T(8,128)(2,1)}, u32[]{:S(2)}) copy-start(bf16[64,16,256]{2,1,0:T(8,128)(2,1)} %param.34) | copy-start | bytes 1572868
  403.7 135.7 %copy-start.6 = (f32[7,7,256]{2,1,0:T(8,128)S(1)}, f32[7,7,256]{2,1,0:T(8,128)}, u32[]{:S(2)}) copy-start(f32[7,7,256]{2,1,0:T(8,128)} %param.40) | copy-start | bytes 150532
  403.7 137.4 %all-to-all-start = ((bf16[4,64,1024]{2,0,1:T(4,128)(2,1)}), bf16[4,64,1024]{2,0,1:T(4,128)(2,1)S(1)}, u32[]{:S(2)}, u32[]{:S(2)}) async-start(bf16[4,64,1024]{2,0,1:T(4,128)(2,1)} %copy.47), calls=%async_computation | async-start | bytes 1048576 | tf_op jit(solution)/shard_map/all_to_all | solution.py:146
  563.1 8.3 %collective-permute-start.2 = (bf16[3,16,256]{2,1,0:T(8,128)(2,1)S(1)}, bf16[3,16,256]{2,1,0:T(8,128)(2,1)S(1)}, u32[]{:S(2)}, u32[]{:S(2)}) collective-permute-start(bf16[3,16,256]{2,1,0:T(8,128)(2,1)S(1)} %get-tuple-element.160), channel_id=1, source_target_pairs={{0,8},{8,16},{16,24},{24,32},{32,40},{40,48},{48,56},{56,64},{64,7... | collective-permute-start | bytes 73736 | tf_op jit(solution)/shard_map/ppermute | solution.py:17
  565.4 7.6 %collective-permute-start.3 = (bf16[3,16,256]{2,1,0:T(8,128)(2,1)S(1)}, bf16[3,16,256]{2,1,0:T(8,128)(2,1)S(1)}, u32[]{:S(2)}, u32[]{:S(2)}) collective-permute-start(bf16[3,16,256]{2,1,0:T(8,128)(2,1)S(1)} %get-tuple-element.159), channel_id=1, source_target_pairs={{8,0},{16,8},{24,16},{32,24},{40,32},{48,40},{56,48},{64,56},{72,6... | collective-permute-start | bytes 73736 | tf_op jit(solution)/shard_map/ppermute | solution.py:20
  574.1 15.7 %collective-permute-start.4 = (bf16[70,3,256]{2,1,0:T(4,128)(2,1)S(1)}, bf16[70,3,256]{2,1,0:T(4,128)(2,1)S(1)}, u32[]{:S(2)}, u32[]{:S(2)}) collective-permute-start(bf16[70,3,256]{2,1,0:T(4,128)(2,1)S(1)} %get-tuple-element.157), channel_id=1, source_target_pairs={{1,0},{2,1},{3,2},{4,3},{5,4},{6,5},{7,6},{9,8},{10,9},{11,10},{12... | collective-permute-start | bytes 322568 | tf_op jit(solution)/shard_map/ppermute | solution.py:20
  585.2 17.2 %collective-permute-start.5 = (bf16[70,3,256]{2,1,0:T(4,128)(2,1)S(1)}, bf16[70,3,256]{2,1,0:T(4,128)(2,1)S(1)}, u32[]{:S(2)}, u32[]{:S(2)}) collective-permute-start(bf16[70,3,256]{2,1,0:T(4,128)(2,1)S(1)} %get-tuple-element.158), channel_id=1, source_target_pairs={{0,1},{1,2},{2,3},{3,4},{4,5},{5,6},{6,7},{8,9},{9,10},{10,11},{11... | collective-permute-start | bytes 322568 | tf_op jit(solution)/shard_map/ppermute | solution.py:17
  (58 other events, 2000.2 us)
Sparse Core Ops, SparseCore 0:
  9.5 127.7 all-gather.5
  139.5 118.6 all-gather.3
  260.4 140.4 all-gather.7
